TPU v7x, 256 devices: a whole 4x4x8 slice. The times are simulated.
256 devices in a mesh: seq: 32 (over x, z), tensor: 8 (over y, core).
Axes of the slice: x: 4, y: 4, z: 8, core: 2. Of those that a mesh axis runs over, the one named last changes fastest.
Arguments:
- queries: bfloat16 [10240, 4096], P('seq', 'tensor'), may hold values from -8 to 8
- key_rows: bfloat16 [10240, 1024], P('seq', 'tensor'), may hold values from -8 to 8
- value_rows: bfloat16 [10240, 1024], P('seq', 'tensor'), may hold values from -6 to 6
- out_weight: bfloat16 [4096, 8192], P('tensor', 'seq'), may hold values from -0.09375 to 0.09375
- residual_in: bfloat16 [10240, 8192], P('seq'), may hold values from -0.1796875 to 0.1796875
- norm_gain: bfloat16 [8192], replicated, may hold values from 0.099609375 to 1.8984375
- prompt_lengths: int32 [18], replicated, may hold values from 1 to 5120, 10240 in all
Outputs:
- normed: bfloat16 [10240, 8192], P('seq')
- cache_keys: bfloat16 [22528, 1024], P('seq', 'tensor')
- cache_values: bfloat16 [22528, 1024], P('seq', 'tensor')
Inputs may be any that keep to these rules, and one draw needn't show every extreme that they name: `prompt_lengths`: the 18 lengths sum to 10240, and the largest is 5120.
All inputs are finite; a program needn't handle non-finite values.
Results may differ from a plain program's by a relative error of at most 0.019.
Values may be sent and summed in bfloat16 or wider, within the bound.
No kernel may reach another device: no remote copies, remote signals or barrier semaphores. Data moves between devices by JAX's collectives and lax.ppermute only.
A program may use at most 192 MiB of HBM per device.

v0:
```python
import math
import jax
import jax.numpy as jnp
from jax import lax
from jax.sharding import PartitionSpec as P

HD = 128
PAGE = 128
SLOT_DEV = 704


def position_of(stored, per_device, devices):
    half_block = per_device // 2
    device = stored // per_device
    offset = stored % per_device
    return jnp.where(
        offset < half_block,
        device * half_block + offset,
        (2 * devices - 1 - device) * half_block + offset - half_block,
    )


def stored_row(position, per_device, devices):
    half_block = per_device // 2
    block_index = position // half_block
    device = jnp.where(block_index < devices, block_index, 2 * devices - 1 - block_index)
    offset = position % half_block + jnp.where(block_index < devices, 0, half_block)
    return device * per_device + offset


def segment_of(position, lengths):
    doc_ends = jnp.cumsum(lengths, dtype=jnp.int32)
    return jnp.sum(
        (position[:, None] >= doc_ends[None, :]).astype(jnp.int32), axis=1, dtype=jnp.int32
    )


def slot_source(slot_ids, lengths, page_size):
    padded = (lengths + page_size - 1) // page_size * page_size
    page_ends = jnp.cumsum(padded, dtype=jnp.int32)
    page_starts = page_ends - padded
    doc_ends = jnp.cumsum(lengths, dtype=jnp.int32)
    doc_starts = doc_ends - lengths
    prompt = jnp.sum(
        (slot_ids[:, None] >= page_ends[None, :]).astype(jnp.int32), axis=1, dtype=jnp.int32
    )
    clipped = jnp.minimum(prompt, lengths.shape[0] - 1)
    within = slot_ids - jnp.take(page_starts, clipped)
    is_live = (prompt < lengths.shape[0]) & (within < jnp.take(lengths, clipped))
    return (jnp.take(doc_starts, clipped) + within, is_live)


def body(queries, key_rows, value_rows, out_weight, residual_in, norm_gain, prompt_lengths):
    seq_count = lax.axis_size("seq")
    seq_index = lax.axis_index("seq")
    per_device = queries.shape[0]
    kv_local = key_rows.shape[1] // HD
    group_size = queries.shape[1] // (kv_local * HD)
    score_scale = 1.0 / math.sqrt(HD)
    local_rows = jnp.arange(per_device, dtype=jnp.int32) + seq_index * per_device
    my_position = position_of(local_rows, per_device, seq_count)
    my_segment = segment_of(my_position, prompt_lengths)
    grouped = queries.reshape(per_device, kv_local, group_size, HD)
    key_piece = lax.all_gather(key_rows, "seq", axis=0, tiled=True)
    value_piece = lax.all_gather(value_rows, "seq", axis=0, tiled=True)
    piece_rows = key_piece.shape[0]
    key_position = position_of(jnp.arange(piece_rows, dtype=jnp.int32), per_device, seq_count)
    key_segment = segment_of(key_position, prompt_lengths)
    allowed = (key_position[None, :] <= my_position[:, None]) & (
        key_segment[None, :] == my_segment[:, None]
    )
    top_old = jnp.full((kv_local, group_size, per_device), -1e30, jnp.float32)
    scores = (
        jnp.einsum(
            "qgjd,kgd->gjqk",
            grouped,
            key_piece.reshape(piece_rows, kv_local, HD),
            preferred_element_type=jnp.float32,
        )
        * score_scale
    )
    scores = jnp.where(allowed, scores, -1e30)
    top_new = jnp.maximum(top_old, jnp.max(scores, axis=-1))
    weights = jnp.where(allowed, jnp.exp(scores - top_new[..., None]), 0.0)
    total_new = jnp.sum(weights, axis=-1)
    accum_new = jnp.einsum(
        "gjqk,kgd->gjqd",
        weights.astype(jnp.bfloat16),
        value_piece.reshape(piece_rows, kv_local, HD),
        preferred_element_type=jnp.float32,
    )
    attended = jnp.transpose(accum_new / total_new[..., None], (2, 0, 1, 3))
    attended = attended.reshape(per_device, -1).astype(jnp.bfloat16)
    partial_value = jnp.dot(
        attended,
        lax.all_gather(out_weight, "seq", axis=1, tiled=True),
        preferred_element_type=jnp.float32,
    )
    projected = lax.psum(partial_value.astype(jnp.bfloat16), "tensor").astype(jnp.float32)
    hidden = residual_in.astype(jnp.float32) + projected
    mean_square = jnp.mean(hidden * hidden, axis=-1, keepdims=True)
    normed = (hidden * lax.rsqrt(mean_square + 1e-05) * norm_gain.astype(jnp.float32)).astype(
        jnp.bfloat16
    )
    slot_ids = seq_index * SLOT_DEV + jnp.arange(SLOT_DEV, dtype=jnp.int32)
    source, is_live = slot_source(slot_ids, prompt_lengths, PAGE)
    target = stored_row(source, per_device, seq_count)
    empty_cache = jnp.zeros((SLOT_DEV, kv_local * HD), jnp.bfloat16)
    key_piece = lax.all_gather(key_rows, "seq", axis=0, tiled=True)
    value_piece = lax.all_gather(value_rows, "seq", axis=0, tiled=True)
    piece_rows = key_piece.shape[0]
    found = is_live & (target >= 0) & (target < piece_rows)
    safe_index = jnp.clip(target, 0, piece_rows - 1)
    cache_keys = jnp.where(found[:, None], jnp.take(key_piece, safe_index, axis=0), empty_cache)
    cache_values = jnp.where(found[:, None], jnp.take(value_piece, safe_index, axis=0), empty_cache)
    return (normed, cache_keys, cache_values)


def solution(mesh):
    return jax.shard_map(
        body,
        mesh=mesh,
        in_specs=(
            P("seq", "tensor"),
            P("seq", "tensor"),
            P("seq", "tensor"),
            P("tensor", "seq"),
            P("seq", None),
            P(),
            P(),
        ),
        out_specs=(P("seq", None), P("seq", "tensor"), P("seq", "tensor")),
        check_vma=False,
    )
```

profile of v0, /device:TPU:1, one launch (start us, length us, event | category | flops | bytes accessed | tf_op | source)
XLA Modules:
  0.0 381.7 jit_solution(8324192015222926720)
XLA Ops:
  7.2 0.7 all-gather.4.cloned.1.call-update
  8.0 0.7 all-gather.6.cloned.1.call-update
  8.7 0.7 all-gather.8.cloned.1.call-update
  9.4 0.7 copy.17
  10.5 0.2 convert_reduce_fusion
  10.8 4.6 %compare_and_fusion = pred[320,10240]{1,0:T(8,128)(4,1)} fusion(s32[10240]{0:T(1024)S(1)} %convert_reduce_fusion, s32[10240]{0:T(1024)S(1)} %fusion.38, s32[320]{0:T(512)S(1)} %convert_reduce_fusion.2, s32[320]{0:T(512)S(1)} %add_select_fusion.5), kind=kLoop, calls=%fused_computation.10 | loop fusion | flops 9830400 | bytes 3361280 | tf_op jit(solution)/shard_map/and | solution.py:69
  15.3 74.5 %all-gather.4.cloned.1.call-done = bf16[10240,128]{1,0:T(8,128)(2,1)} async-done(((bf16[320,128]{1,0:T(8,128)(2,1)}), bf16[10240,128]{1,0:T(8,128)(2,1)}) %all-gather.4.cloned.1.call-update) | async-done | bytes 2621456 | tf_op jit(solution)/shard_map/all_gather | solution.py:64
  89.8 22.6 %fusion = (f32[4,320]{1,0:T(4,128)S(1)}, f32[10240,320,4]{0,1,2:T(8,128)}) fusion(pred[320,10240]{1,0:T(8,128)(4,1)} %compare_and_fusion, bf16[10240,128]{1,0:T(8,128)(2,1)} %all-gather.4.cloned.1.call-done, bf16[320,512]{1,0:T(8,128)(2,1)S(1)} %copy-done), kind=kOutput, calls=%fused_computation.4 | convolution fusion | flops 3394763520 | bytes 58659840 | tf_op jit(solution)/shard_map/qgjd,kgd->gjqk/dot_general | solution.py:74
  112.4 22.7 %fusion.1 = f32[4,320]{1,0:T(4,128)S(1)} fusion(f32[10240,320,4]{0,1,2:T(8,128)} %get-tuple-element.66, f32[4,320]{1,0:T(4,128)S(1)} %broadcast_maximum_fusion, pred[320,10240]{1,0:T(8,128)(4,1)} %compare_and_fusion), kind=kLoop, calls=%fused_computation.5 | loop fusion | flops 65534720 | bytes 55715840 | tf_op jit(solution)/shard_map/reduce_sum | solution.py:85
  135.1 33.1 %all-gather.6.cloned.1.call-done = bf16[10240,128]{1,0:T(8,128)(2,1)} async-done(((bf16[320,128]{1,0:T(8,128)(2,1)}), bf16[10240,128]{1,0:T(8,128)(2,1)}) %all-gather.6.cloned.1.call-update) | async-done | bytes 2621456 | tf_op jit(solution)/shard_map/all_gather | solution.py:65
  168.2 23.3 %fusion.20 = bf16[320,1,4,128]{3,0,2,1:T(8,128)(2,1)S(1)} fusion(bf16[10240,128]{1,0:T(8,128)(2,1)} %all-gather.6.cloned.1.call-done, f32[10240,320,4]{0,1,2:T(8,128)} %get-tuple-element.66, f32[4,320]{1,0:T(4,128)S(1)} %broadcast_maximum_fusion, pred[320,10240]{1,0:T(8,128)(4,1)} %compare_and_fusion, f32[4,320]{1,0:T(4,128)S(1)} %fusion.1), kind=kOutput, calls=%fused_computation.20 | convolution fusion | flops 3421306880 | bytes 58664960 | tf_op jit(solution)/shard_map/gjqk,kgd->gjqd/dot_general | solution.py:86
  191.6 0.3 copy.19
  191.9 80.5 %all-gather.8.cloned.1.call-done = bf16[512,8192]{1,0:T(8,128)(2,1)} async-done(((bf16[512,256]{1,0:T(8,128)(2,1)}), bf16[512,8192]{1,0:T(8,128)(2,1)}) %all-gather.8.cloned.1.call-update) | async-done | bytes 8388624 | tf_op jit(solution)/shard_map/all_gather | solution.py:96
  272.4 8.1 %convolution_convert_fusion = bf16[320,8192]{1,0:T(8,128)(2,1)} fusion(bf16[512,8192]{1,0:T(8,128)(2,1)} %all-gather.8.cloned.1.call-done, bf16[40,8,4,128]{3,2,1,0:T(4,128)(2,1)S(1)} %bitcast.120), kind=kOutput, calls=%fused_computation.11 | convolution fusion | flops 2686976000 | bytes 13959168 | tf_op jit(solution)/shard_map/dot_general | solution.py:94
  280.9 0.7 fusion.58
  281.6 0.7 fusion.57
  282.3 0.7 fusion.55
  283.1 33.8 %compare_and_fusion.3 = (pred[704]{0:T(1024)(128)(4,1)S(1)}, s32[704]{0:T(1024)S(1)}) fusion(s32[704]{0:T(1024)S(1)} %convert_reduce_fusion.1, s32[]{:T(128)} %bitcast.44, s32[]{:T(128)} %bitcast.43, s32[]{:T(128)} %bitcast.42, s32[]{:T(128)} %bitcast.41, s32[]{:T(128)} %bitcast.40, s32[]{:T(128)} %bitcast.39, s32[]{:T(128)} %bitcast.38, s32[]{:T(128)} %bitcast.37, ...), kind=kLoop, calls=%fused_computation.64 | loop fusion | flops 75328 | bytes 6556 | tf_op jit(solution)/shard_map/and | solution.py:112
  317.0 2.0 gather_fusion
  319.0 3.9 %gather_fusion.1 = bf16[704,128]{1,0:T(8,128)(2,1)S(1)} fusion(bf16[10240,128]{1,0:T(8,128)(2,1)} %all-gather.6.cloned.1.call-done, s32[1024]{0:T(1024)S(1)} %pad_clamp_fusion), kind=kCustom, calls=%fused_computation.1.clone | custom fusion | bytes 363264 | tf_op jit(solution)/shard_map/jit(_take)/gather | solution.py:115
  322.9 1.0 select_select_fusion
  323.9 38.1 %all-reduce.2.cloned.1.call-done = bf16[320,8192]{1,0:T(8,128)(2,1)} async-done(((bf16[320,8192]{1,0:T(8,128)(2,1)}), bf16[320,8192]{1,0:T(8,128)(2,1)}) %all-reduce.2.cloned.1.call-update) | async-done | bytes 5242896 | tf_op jit(solution)/shard_map/psum | solution.py:99
  362.0 6.0 %multiply_reduce_fusion = f32[320]{0:T(512)S(1)} fusion(bf16[320,8192]{1,0:T(8,128)(2,1)} %all-reduce.2.cloned.1.call-done, bf16[320,8192]{1,0:T(8,128)(2,1)} %param.15), kind=kLoop, calls=%fused_computation.13 | loop fusion | flops 13106880 | bytes 10487040 | tf_op jit(solution)/shard_map/reduce_sum | solution.py:101
  368.0 7.1 %multiply_convert_fusion = bf16[320,8192]{1,0:T(8,128)(2,1)} fusion(bf16[320,8192]{1,0:T(8,128)(2,1)S(1)} %copy-done.2, bf16[320,8192]{1,0:T(8,128)(2,1)} %param.15, f32[8192]{0:T(1024)S(1)} %convert_element_type.49, f32[320]{0:T(512)S(1)} %add_rsqrt_fusion), kind=kLoop, calls=%fused_computation.12 | loop fusion | flops 15728640 | bytes 15762688 | tf_op jit(solution)/shard_map/convert_element_type | solution.py:102
  (35 shorter events, 0.9 us)
Async XLA Ops:
  7.2 82.6 %copy-start = (bf16[320,512]{1,0:T(8,128)(2,1)S(1)}, bf16[320,512]{1,0:T(8,128)(2,1)}, u32[]{:S(2)}) copy-start(bf16[320,512]{1,0:T(8,128)(2,1)} %param.11) | copy-start | bytes 983044
  7.2 82.6 %all-gather.4.cloned.1.call-start = ((), (), s32[]{:S(2)}) async-start(), calls=%async_computation | async-start | bytes 2703360 | tf_op jit(solution)/shard_map/all_gather | solution.py:64
  7.9 160.3 %all-gather.6.cloned.1.call-start = ((), (), s32[]{:S(2)}) async-start(), calls=%async_computation.1 | async-start | bytes 2703360 | tf_op jit(solution)/shard_map/all_gather | solution.py:65
  8.7 263.7 %all-gather.8.cloned.1.call-start = ((), (), s32[]{:S(2)}) async-start(), calls=%async_computation.2 | async-start | bytes 8650752 | tf_op jit(solution)/shard_map/all_gather | solution.py:96
  9.4 352.6 %all-reduce.2.cloned.1.call-start = ((), (), s32[]{:S(2)}) async-start(), calls=%async_computation.3 | async-start | bytes 10485760 | tf_op jit(solution)/shard_map/psum | solution.py:99
  191.9 88.7 %copy-start.4 = (s32[18]{0:T(128)S(1)}, s32[18]{0:T(128)}, u32[]{:S(2)}) copy-start(s32[18]{0:T(128)} %param.17) | copy-start | bytes 220
  191.9 89.0 %copy-start.5 = (bf16[8192]{0:T(1024)(128)(2,1)S(1)}, bf16[8192]{0:T(1024)(128)(2,1)}, u32[]{:S(2)}) copy-start(bf16[8192]{0:T(1024)(128)(2,1)} %param.16) | copy-start | bytes 49156
  272.4 44.6 %copy-start.3 = (bf16[10240,128]{1,0:T(8,128)(2,1)S(1)}, bf16[10240,128]{1,0:T(8,128)(2,1)}, u32[]{:S(2)}) copy-start(bf16[10240,128]{1,0:T(8,128)(2,1)} %all-gather.4.cloned.1.call-done) | copy-start | bytes 7864324
  362.0 6.0 %copy-start.2 = (bf16[320,8192]{1,0:T(8,128)(2,1)S(1)}, bf16[320,8192]{1,0:T(8,128)(2,1)}, u32[]{:S(2)}) copy-start(bf16[320,8192]{1,0:T(8,128)(2,1)} %all-reduce.2.cloned.1.call-done) | copy-start | bytes 15728644
  362.0 13.1 %copy-start.1 = (bf16[320,512]{1,0:T(8,128)(2,1)S(1)}, bf16[320,512]{1,0:T(8,128)(2,1)}, u32[]{:S(2)}) copy-start(bf16[320,512]{1,0:T(8,128)(2,1)} %param.11) | copy-start | bytes 983044
Sparse Core Ops, SparseCore 0:
  10.6 79.1 all-gather.3
  92.4 75.8 all-gather.5
  170.7 101.6 all-gather.7
  280.7 81.3 all-reduce.1
where the time goes:
time: 382 us
  waiting for transfers between devices  228 us (60%)
  other arithmetic  76 us (20%)
  matrix products  54.1 us (14%)
  between operations  13.9 us (4%)
  local copies, waits for them, and re-layouts  9.24 us (2%)
    all_gather x1, waiting for transfers between devices, body(): lax.all_gather(out_weight, 'seq', axis=1, tiled=True)  80.5 us
    all_gather x1, waiting for transfers between devices, body(): key_piece = lax.all_gather(key_rows, 'seq', axis=0, tiled=True)  74.5 us
    psum x1, waiting for transfers between devices, body(): lax.psum(partial_value.astype(jnp.bfloat16), 'tensor').astype(jnp.float32)  38.1 us
    and x1, other arithmetic, body(): found = is_live & (target >= 0) & (target < piece_rows)  33.8 us
    all_gather x1, waiting for transfers between devices, body(): value_piece = lax.all_gather(value_rows, 'seq', axis=0, tiled=True)  33.1 us
    dot_general x1, matrix products, body(): jnp.einsum('gjqk,kgd->gjqd', weights.astype(jnp.bfloat16), value_piece.re...  23.3 us
    reduce_sum x1, other arithmetic, body(): total_new = jnp.sum(weights, axis=-1)  22.7 us
    dot_general x1, matrix products, body(): jnp.einsum('qgjd,kgd->gjqk', grouped, key_piece.reshape(piece_rows, kv_lo...  22.6 us
  transfers between devices with their start and end apart: 4, of which 4 were waited for; matrix products, arithmetic and copies ran while one was open for 31% of the time, Pallas kernels for 0%

commit v1 on v0

--- a/solution.py
+++ b/solution.py
@@ -61,8 +61,11 @@
     my_position = position_of(local_rows, per_device, seq_count)
     my_segment = segment_of(my_position, prompt_lengths)
     grouped = queries.reshape(per_device, kv_local, group_size, HD)
-    key_piece = lax.all_gather(key_rows, "seq", axis=0, tiled=True)
-    value_piece = lax.all_gather(value_rows, "seq", axis=0, tiled=True)
+    key_piece, value_piece = jnp.split(
+        lax.all_gather(jnp.concatenate([key_rows, value_rows], axis=1), "seq", axis=0, tiled=True),
+        [key_rows.shape[1]],
+        axis=1,
+    )
     piece_rows = key_piece.shape[0]
     key_position = position_of(jnp.arange(piece_rows, dtype=jnp.int32), per_device, seq_count)
     key_segment = segment_of(key_position, prompt_lengths)

time: 382 us -> 462 us (1.21)
  waiting for transfers between devices: 228 us -> 305 us
    all_gather x0 -> x1, waiting for transfers between devices: none -> 80.8 us  [body(): lax.all_gather(jnp.concatenate([key_rows, value_rows], axis=1), 'seq', ax...]
    all_gather x1, waiting for transfers between devices: 80.5 us -> 34.1 us  [body(): lax.all_gather(out_weight, 'seq', axis=1, tiled=True)]
    psum x1, waiting for transfers between devices: 38.1 us -> 79.8 us  [body(): lax.psum(partial_value.astype(jnp.bfloat16), 'tensor').astype(jnp.float32)]
    all_gather x1, waiting for transfers between devices: 33.1 us -> 74.5 us  [body(): value_piece = lax.all_gather(value_rows, 'seq', axis=0, tiled=True)]
    all_gather x1, waiting for transfers between devices: 74.5 us -> 33.7 us  [body(): key_piece = lax.all_gather(key_rows, 'seq', axis=0, tiled=True)]
  transfers between devices with their start and end apart: 4 -> 5, of which waited for: 4 -> 5; matrix products, arithmetic and copies ran while one was open for 31% -> 28% of each run, Pallas kernels for 0% -> 0%
where the time goes in v1:
time: 462 us
  waiting for transfers between devices  305 us (66%)
  other arithmetic  77.7 us (17%)
  matrix products  54.1 us (12%)
  between operations  13.9 us (3%)
  local copies, waits for them, and re-layouts  11 us (2%)
    all_gather x1, waiting for transfers between devices, body(): lax.all_gather(jnp.concatenate([key_rows, value_rows], axis=1), 'seq', ax...  80.8 us
    psum x1, waiting for transfers between devices, body(): lax.psum(partial_value.astype(jnp.bfloat16), 'tensor').astype(jnp.float32)  79.8 us
    all_gather x1, waiting for transfers between devices, body(): value_piece = lax.all_gather(value_rows, 'seq', axis=0, tiled=True)  74.5 us
    all_gather x1, waiting for transfers between devices, body(): lax.all_gather(out_weight, 'seq', axis=1, tiled=True)  34.1 us
    and x1, other arithmetic, body(): found = is_live & (target >= 0) & (target < piece_rows)  33.8 us
    all_gather x1, waiting for transfers between devices, body(): key_piece = lax.all_gather(key_rows, 'seq', axis=0, tiled=True)  33.7 us
    dot_general x1, matrix products, body(): jnp.einsum('gjqk,kgd->gjqd', weights.astype(jnp.bfloat16), value_piece.re...  23.3 us
    dot_general x1, matrix products, body(): jnp.einsum('qgjd,kgd->gjqk', grouped, key_piece.reshape(piece_rows, kv_lo...  22.9 us
  transfers between devices with their start and end apart: 5, of which 5 were waited for; matrix products, arithmetic and copies ran while one was open for 28% of the time, Pallas kernels for 0%

profile of v1, /device:TPU:1, one launch (start us, length us, event | category | flops | bytes accessed | tf_op | source)
XLA Modules:
  0.0 461.6 jit_solution(11689171742592440987)
XLA Ops:
  7.2 1.6 pad_maximum_fusion
  9.0 0.7 all-gather.7.cloned.1.call-update
  9.7 0.7 all-gather.9.cloned.1.call-update
  10.4 0.5 all-gather.11.cloned.1.call-update
  11.1 0.7 copy.17
  12.3 4.6 compare_and_fusion
  16.9 80.8 %all-gather.5.cloned.1.call-done = bf16[10240,256]{1,0:T(8,128)(2,1)} async-done(((bf16[320,256]{1,0:T(8,128)(2,1)}), bf16[10240,256]{1,0:T(8,128)(2,1)}) %all-gather.5.cloned.1.call-update) | async-done | bytes 5242896 | tf_op jit(solution)/shard_map/all_gather | solution.py:65
  97.7 22.9 %fusion = (f32[4,320]{1,0:T(4,128)S(1)}, f32[10240,320,4]{0,1,2:T(8,128)}) fusion(pred[320,10240]{1,0:T(8,128)(4,1)} %compare_and_fusion, bf16[10240,256]{1,0:T(8,128)(2,1)} %all-gather.5.cloned.1.call-done, bf16[320,512]{1,0:T(8,128)(2,1)S(1)} %copy-done), kind=kOutput, calls=%fused_computation.4 | convolution fusion | flops 3394763520 | bytes 58659840 | tf_op jit(solution)/shard_map/qgjd,kgd->gjqk/dot_general | solution.py:77
  120.5 22.7 %fusion.1 = f32[4,320]{1,0:T(4,128)S(1)} fusion(f32[10240,320,4]{0,1,2:T(8,128)} %get-tuple-element.66, f32[4,320]{1,0:T(4,128)S(1)} %broadcast_maximum_fusion, pred[320,10240]{1,0:T(8,128)(4,1)} %compare_and_fusion), kind=kLoop, calls=%fused_computation.5 | loop fusion | flops 65534720 | bytes 55715840 | tf_op jit(solution)/shard_map/reduce_sum | solution.py:88
  143.3 23.3 %fusion.14 = bf16[320,1,4,128]{3,0,2,1:T(8,128)(2,1)S(1)} fusion(bf16[10240,256]{1,0:T(8,128)(2,1)} %all-gather.5.cloned.1.call-done, f32[10240,320,4]{0,1,2:T(8,128)} %get-tuple-element.66, f32[4,320]{1,0:T(4,128)S(1)} %broadcast_maximum_fusion, pred[320,10240]{1,0:T(8,128)(4,1)} %compare_and_fusion, f32[4,320]{1,0:T(4,128)S(1)} %fusion.1), kind=kOutput, calls=%fused_computation.20 | convolution fusion | flops 3421306880 | bytes 58664960 | tf_op jit(solution)/shard_map/gjqk,kgd->gjqd/dot_general | solution.py:89
  166.8 34.1 %all-gather.7.cloned.1.call-done = bf16[512,8192]{1,0:T(8,128)(2,1)} async-done(((bf16[512,256]{1,0:T(8,128)(2,1)}), bf16[512,8192]{1,0:T(8,128)(2,1)}) %all-gather.7.cloned.1.call-update) | async-done | bytes 8388624 | tf_op jit(solution)/shard_map/all_gather | solution.py:99
  200.9 8.0 %convolution_convert_fusion = bf16[320,8192]{1,0:T(8,128)(2,1)} fusion(bf16[512,8192]{1,0:T(8,128)(2,1)} %all-gather.7.cloned.1.call-done, bf16[40,8,4,128]{3,2,1,0:T(4,128)(2,1)S(1)} %bitcast.120), kind=kOutput, calls=%fused_computation.11 | convolution fusion | flops 2686976000 | bytes 13959168 | tf_op jit(solution)/shard_map/dot_general | solution.py:97
  209.2 0.7 fusion.50
  209.9 0.7 fusion.49
  210.7 0.7 fusion.47
  211.5 33.8 %compare_and_fusion.3 = (pred[704]{0:T(1024)(128)(4,1)S(1)}, s32[704]{0:T(1024)S(1)}) fusion(s32[704]{0:T(1024)S(1)} %convert_reduce_fusion.1, s32[]{:T(128)} %bitcast.44, s32[]{:T(128)} %bitcast.43, s32[]{:T(128)} %bitcast.42, s32[]{:T(128)} %bitcast.41, s32[]{:T(128)} %bitcast.40, s32[]{:T(128)} %bitcast.39, s32[]{:T(128)} %bitcast.38, s32[]{:T(128)} %bitcast.37, ...), kind=kLoop, calls=%fused_computation.65 | loop fusion | flops 75328 | bytes 6556 | tf_op jit(solution)/shard_map/and | solution.py:115
  245.3 33.7 %all-gather.9.cloned.1.call-done = bf16[10240,128]{1,0:T(8,128)(2,1)} async-done(((bf16[320,128]{1,0:T(8,128)(2,1)}), bf16[10240,128]{1,0:T(8,128)(2,1)}) %all-gather.9.cloned.1.call-update) | async-done | bytes 2621456 | tf_op jit(solution)/shard_map/all_gather | solution.py:112
  279.0 3.8 gather_fusion
  282.8 74.5 %all-gather.11.cloned.1.call-done = bf16[10240,128]{1,0:T(8,128)(2,1)} async-done(((bf16[320,128]{1,0:T(8,128)(2,1)}), bf16[10240,128]{1,0:T(8,128)(2,1)}) %all-gather.11.cloned.1.call-update) | async-done | bytes 2621456 | tf_op jit(solution)/shard_map/all_gather | solution.py:113
  357.3 3.8 gather_fusion.1
  361.1 1.0 select_select_fusion
  362.1 79.8 %all-reduce.2.cloned.1.call-done = bf16[320,8192]{1,0:T(8,128)(2,1)} async-done(((bf16[320,8192]{1,0:T(8,128)(2,1)}), bf16[320,8192]{1,0:T(8,128)(2,1)}) %all-reduce.2.cloned.1.call-update) | async-done | bytes 5242896 | tf_op jit(solution)/shard_map/psum | solution.py:102
  441.9 6.0 %multiply_reduce_fusion = f32[320]{0:T(512)S(1)} fusion(bf16[320,8192]{1,0:T(8,128)(2,1)} %all-reduce.2.cloned.1.call-done, bf16[320,8192]{1,0:T(8,128)(2,1)} %param.15), kind=kLoop, calls=%fused_computation.13 | loop fusion | flops 13106880 | bytes 10487040 | tf_op jit(solution)/shard_map/reduce_sum | solution.py:104
  447.9 7.1 %multiply_convert_fusion = bf16[320,8192]{1,0:T(8,128)(2,1)} fusion(bf16[320,8192]{1,0:T(8,128)(2,1)S(1)} %copy-done.2, bf16[320,8192]{1,0:T(8,128)(2,1)} %param.15, f32[8192]{0:T(1024)S(1)} %convert_element_type.49, f32[320]{0:T(512)S(1)} %add_rsqrt_fusion), kind=kLoop, calls=%fused_computation.12 | loop fusion | flops 15728640 | bytes 15762688 | tf_op jit(solution)/shard_map/convert_element_type | solution.py:105
  (37 shorter events, 1.5 us)
Async XLA Ops:
  7.2 90.5 %copy-start = (bf16[320,512]{1,0:T(8,128)(2,1)S(1)}, bf16[320,512]{1,0:T(8,128)(2,1)}, u32[]{:S(2)}) copy-start(bf16[320,512]{1,0:T(8,128)(2,1)} %param.11) | copy-start | bytes 983044
  7.2 90.5 %all-gather.5.cloned.1.call-start = ((), (), s32[]{:S(2)}) async-start(), calls=%async_computation | async-start | bytes 5406720 | tf_op jit(solution)/shard_map/all_gather | solution.py:65
  8.9 192.0 %all-gather.7.cloned.1.call-start = ((), (), s32[]{:S(2)}) async-start(), calls=%async_computation.1 | async-start | bytes 8650752 | tf_op jit(solution)/shard_map/all_gather | solution.py:99
  9.7 269.3 %all-gather.9.cloned.1.call-start = ((), (), s32[]{:S(2)}) async-start(), calls=%async_computation.3 | async-start | bytes 2703360 | tf_op jit(solution)/shard_map/all_gather | solution.py:112
  10.4 346.9 %all-gather.11.cloned.1.call-start = ((), (), s32[]{:S(2)}) async-start(), calls=%async_computation.4 | async-start | bytes 2703360 | tf_op jit(solution)/shard_map/all_gather | solution.py:113
  11.0 430.9 %all-reduce.2.cloned.1.call-start = ((), (), s32[]{:S(2)}) async-start(), calls=%async_computation.2 | async-start | bytes 10485760 | tf_op jit(solution)/shard_map/psum | solution.py:102
  166.8 42.1 %copy-start.3 = (s32[18]{0:T(128)S(1)}, s32[18]{0:T(128)}, u32[]{:S(2)}) copy-start(s32[18]{0:T(128)} %param.17) | copy-start | bytes 220
  166.8 42.4 %copy-start.4 = (bf16[8192]{0:T(1024)(128)(2,1)S(1)}, bf16[8192]{0:T(1024)(128)(2,1)}, u32[]{:S(2)}) copy-start(bf16[8192]{0:T(1024)(128)(2,1)} %param.16) | copy-start | bytes 49156
  441.9 6.0 %copy-start.2 = (bf16[320,8192]{1,0:T(8,128)(2,1)S(1)}, bf16[320,8192]{1,0:T(8,128)(2,1)}, u32[]{:S(2)}) copy-start(bf16[320,8192]{1,0:T(8,128)(2,1)} %all-reduce.2.cloned.1.call-done) | copy-start | bytes 15728644
  441.9 13.1 %copy-start.1 = (bf16[320,512]{1,0:T(8,128)(2,1)S(1)}, bf16[320,512]{1,0:T(8,128)(2,1)}, u32[]{:S(2)}) copy-start(bf16[320,512]{1,0:T(8,128)(2,1)} %param.11) | copy-start | bytes 983044
Sparse Core Ops, SparseCore 0:
  11.2 86.4 all-gather.4
  100.1 100.7 all-gather.6
  203.5 75.4 all-gather.8
  281.4 75.8 all-gather.10
  360.1 81.7 all-reduce.1
